TPU v7x, 32 devices: a whole 2x2x4 slice. The times are simulated.
32 devices in a mesh: tm: 8 (over z, core), space: 4 (over y, x).
Axes of the slice: x: 2, y: 2, z: 4, core: 2. Of those that a mesh axis runs over, the one named last changes fastest.
Arguments:
- volumes: float32 [8, 64, 512, 128], P('tm', 'space'), may hold values from -12 to 12
Outputs:
- corrected: float32 [8, 64, 512, 128], P('tm', 'space')
- shifts: float32 [8, 3], P('tm')
All inputs are finite; a program needn't handle non-finite values.
Results may differ from a plain program's by a relative error of at most 0.0003.
Values sent between devices are 32-bit elements; how exact they have to be, the bound alone decides.
No kernel may reach another device: no remote copies, remote signals or barrier semaphores. Data moves between devices by JAX's collectives and lax.ppermute only.
A program may use at most 128 MiB of HBM per device.

v0:
```python
import math
import jax
import jax.numpy as jnp
from jax import lax
from jax.sharding import PartitionSpec as P

X = 512
Y = 128
Z = 64
ITERS = 2
precise = lax.Precision.HIGHEST
sharpness = 256.0
floor_share = 0.05


def dft_tables(length):
    indices = jnp.arange(length, dtype=jnp.int32)
    products = indices[:, None] * indices[None, :] % length
    angles = products.astype(jnp.float32) * (2.0 * math.pi / length)
    return (jnp.cos(angles), jnp.sin(angles))


def signed_freq(indices, length):
    wrapped = jnp.where(indices < length // 2, indices, indices - length)
    return jnp.where(indices == length // 2, 0, wrapped).astype(jnp.float32)


def centred(indices, length):
    return ((indices + length // 2) % length - length // 2).astype(jnp.float32)


def mix_z(table, data):
    return jnp.einsum("kz,vz...->vk...", table, data, precision=precise)


def mix_x(table, data):
    return jnp.einsum("kx,vzx...->vzk...", table, data, precision=precise)


def mix_y(data, table):
    return jnp.dot(data, table, precision=precise)


def forward(volume, tables):
    cos_x, sin_x, cos_y, sin_y, cos_z, sin_z = tables
    real_x = mix_x(cos_x, volume)
    imag_x = -mix_x(sin_x, volume)
    real_y = mix_y(real_x, cos_y) + mix_y(imag_x, sin_y)
    imag_y = mix_y(imag_x, cos_y) - mix_y(real_x, sin_y)
    real_p, imag_p = (
        lax.all_to_all(real_y, "space", split_axis=2, concat_axis=1, tiled=True),
        lax.all_to_all(imag_y, "space", split_axis=2, concat_axis=1, tiled=True),
    )
    real_z = mix_z(cos_z, real_p) + mix_z(sin_z, imag_p)
    imag_z = mix_z(cos_z, imag_p) - mix_z(sin_z, real_p)
    return (real_z, imag_z)


def inverse(spectrum, tables):
    cos_x, sin_x, cos_y, sin_y, cos_z, sin_z = tables
    norming = 1.0 / (X * Y * Z)
    real_in, imag_in = spectrum
    real_z = mix_z(cos_z, real_in) - mix_z(sin_z, imag_in)
    imag_z = mix_z(sin_z, real_in) + mix_z(cos_z, imag_in)
    real_y = mix_y(real_z, cos_y) - mix_y(imag_z, sin_y)
    imag_y = mix_y(real_z, sin_y) + mix_y(imag_z, cos_y)
    real_s, imag_s = (
        lax.all_to_all(real_y, "space", split_axis=1, concat_axis=2, tiled=True),
        lax.all_to_all(imag_y, "space", split_axis=1, concat_axis=2, tiled=True),
    )
    return (mix_x(cos_x, real_s) - mix_x(sin_x, imag_s)) * norming


def split_pairs(spectrum):
    return [(spectrum[0], spectrum[1])]


def join_pairs(pairs):
    return (pairs[0][0], pairs[0][1])


def y_frequencies():
    return [signed_freq(jnp.arange(Y, dtype=jnp.int32), Y)]


def template_sum(spectrum):
    return lax.psum((jnp.sum(spectrum[0], axis=0), jnp.sum(spectrum[1], axis=0)), "tm")


def weight_moments(weights, coords):
    coord_z, coord_x, coord_y = coords
    weight_sum = jnp.sum(weights, axis=(1, 2, 3))
    moment_z = jnp.sum(jnp.sum(weights, axis=(2, 3)) * coord_z[None, :], axis=1)
    moment_x = jnp.sum(jnp.sum(weights, axis=(1, 3)) * coord_x[None, :], axis=1)
    moment_y = jnp.sum(jnp.sum(weights, axis=(1, 2)) * coord_y[None, :], axis=1)
    return (weight_sum, jnp.stack([moment_z, moment_x, moment_y], axis=1))


def centroid(scores, coords):
    local_top = jnp.max(scores, axis=(1, 2, 3))
    top_score = lax.pmax(local_top, "space")
    weights = jnp.exp(scores - top_score[:, None, None, None])
    weight_sum, moments = weight_moments(weights, coords)
    weight_sum, moments = lax.psum((weight_sum, moments), "space")
    return moments / weight_sum[:, None]


def apply_ramp(real_in, imag_in, shifts, freq_z, freq_x, freq_y):
    phases = (
        2.0
        * math.pi
        * (
            freq_z[None, :, None] * (shifts[:, 0] / Z)[:, None, None]
            + freq_x[None, None, :] * (shifts[:, 1] / X)[:, None, None]
        )
    )
    phases = (
        phases[..., None]
        + 2.0 * math.pi * freq_y[None, None, None, :] * (shifts[:, 2] / Y)[:, None, None, None]
    )
    cosine = jnp.cos(phases)
    sine = jnp.sin(phases)
    return (real_in * cosine - imag_in * sine, real_in * sine + imag_in * cosine)


def whiten(spec_re, spec_im, tmpl_re, tmpl_im):
    prod_re = spec_re * tmpl_re + spec_im * tmpl_im
    prod_im = spec_im * tmpl_re - spec_re * tmpl_im
    divisor = jnp.maximum(
        jnp.sqrt(prod_re * prod_re + prod_im * prod_im), floor_share * (X * Y * Z)
    )
    return (prod_re / divisor, prod_im / divisor)


def body(volumes):
    position = lax.axis_index("space")
    slab_depth = volumes.shape[1]
    pencil = X // lax.axis_size("space")
    frames = volumes.shape[0] * lax.axis_size("tm")
    tables = dft_tables(X) + dft_tables(Y) + dft_tables(Z)
    z_index = position * slab_depth + jnp.arange(slab_depth, dtype=jnp.int32)
    x_index = position * pencil + jnp.arange(pencil, dtype=jnp.int32)
    coords = (
        centred(z_index, Z),
        centred(jnp.arange(X, dtype=jnp.int32), X),
        centred(jnp.arange(Y, dtype=jnp.int32), Y),
    )
    freq_z = signed_freq(jnp.arange(Z, dtype=jnp.int32), Z)
    freq_x = signed_freq(x_index, X)
    freq_ys = y_frequencies()
    spectrum = forward(volumes, tables)
    spec_pairs = split_pairs(spectrum)
    shifted = spectrum
    for iteration in range(ITERS):
        summed = template_sum(shifted)
        template = tuple((part[None] / frames for part in summed))
        tmpl_pairs = split_pairs(template)
        white_pairs = [
            whiten(spec_pairs[0][0], spec_pairs[0][1], tmpl_pairs[0][0], tmpl_pairs[0][1])
        ]
        correlation = inverse(join_pairs(white_pairs), tables)
        shifts = centroid(sharpness * correlation, coords)
        ramped = [
            apply_ramp(spec_pairs[0][0], spec_pairs[0][1], shifts, freq_z, freq_x, freq_ys[0])
        ]
        shifted = join_pairs(ramped)
    corrected = inverse(shifted, tables)
    return (corrected, shifts)


def solution(mesh):
    in_specs = (P("tm", "space", None, None),)
    out_specs = (P("tm", "space", None, None), P("tm", None))
    return jax.shard_map(body, mesh=mesh, in_specs=in_specs, out_specs=out_specs, check_vma=False)
```

profile of v0, /device:TPU:0, one launch (start us, length us, event | category | flops | bytes accessed | tf_op | source)
XLA Modules:
  0.0 1235.6 jit_solution(4220639546576311592)
XLA Ops:
  7.2 13.2 %fusion.46 = f32[512,16,128]{2,0,1:T(8,128)S(1)} fusion(f32[1,16,512,128]{3,2,1,0:T(8,128)} %param.1), kind=kOutput, calls=%fused_computation.58 | convolution fusion | flops 6446120960 | bytes 8388608 | tf_op jit(solution)/shard_map/kx,vzx...->vzk.../dot_general | solution.py:37
  20.4 11.1 fusion.44
  63.7 34.3 %all-to-all-done = f32[1,16,512,128]{3,1,0,2:T(8,128)} async-done(((f32[1,16,512,128]{3,1,0,2:T(8,128)}), f32[1,16,512,128]{3,1,0,2:T(8,128)}, u32[]{:S(2)}, u32[]{:S(2)}) %all-to-all-start) | async-done | bytes 4194336 | tf_op jit(solution)/shard_map/all_to_all | solution.py:51
  113.4 36.6 %all-to-all-done.1 = f32[1,16,512,128]{3,1,0,2:T(8,128)} async-done(((f32[1,16,512,128]{3,1,0,2:T(8,128)}), f32[1,16,512,128]{3,1,0,2:T(8,128)}, u32[]{:S(2)}, u32[]{:S(2)}) %all-to-all-start.1) | async-done | bytes 4194336 | tf_op jit(solution)/shard_map/all_to_all | solution.py:52
  168.3 176.1 %all-reduce.9.cloned.1.call-done = (f32[64,128,128]{2,0,1:T(8,128)}, f32[64,128,128]{2,0,1:T(8,128)}) async-done(((f32[64,128,128]{2,0,1:T(8,128)}, f32[64,128,128]{2,0,1:T(8,128)}), (f32[64,128,128]{2,0,1:T(8,128)}, f32[64,128,128]{2,0,1:T(8,128)})) %all-reduce.9.cloned.1.call-update) | async-done | bytes 8388624 | tf_op jit(solution)/shard_map/psum | solution.py:87
  344.4 10.4 fusion.34
  354.8 8.4 fusion.28
  363.2 6.3 fusion.26
  369.6 6.2 subtract_bitcast_fusion.5
  375.8 6.4 add_bitcast_fusion.5
  382.2 7.1 fusion.68
  389.3 8.2 add_bitcast_fusion.4
  402.8 8.8 fusion.70
  411.6 8.2 subtract_bitcast_fusion.4
  419.8 30.4 %all-to-all-done.3 = f32[1,64,128,128]{3,2,0,1:T(8,128)} async-done(((f32[1,64,128,128]{3,2,0,1:T(8,128)}), f32[1,64,128,128]{3,2,0,1:T(8,128)}, u32[]{:S(2)}, u32[]{:S(2)}) %all-to-all-start.3) | async-done | bytes 4194336 | tf_op jit(solution)/shard_map/all_to_all | solution.py:69
  465.8 36.2 %all-to-all-done.2 = f32[1,64,128,128]{3,2,0,1:T(8,128)} async-done(((f32[1,64,128,128]{3,2,0,1:T(8,128)}), f32[1,64,128,128]{3,2,0,1:T(8,128)}, u32[]{:S(2)}, u32[]{:S(2)}) %all-to-all-start.2) | async-done | bytes 4194336 | tf_op jit(solution)/shard_map/all_to_all | solution.py:68
  512.9 12.9 %fusion.121 = f32[16,128,512]{2,1,0:T(8,128)S(1)} fusion(f32[16,512,128]{1,2,0:T(8,128)} %reshape.463), kind=kOutput, calls=%fused_computation.135 | convolution fusion | flops 6446120960 | bytes 8388608 | tf_op jit(solution)/shard_map/kx,vzx...->vzk.../dot_general | solution.py:37
  525.9 13.1 %fusion.407 = (f32[]{:T(128)}, f32[16,128,512]{2,1,0:T(8,128)}) fusion(f32[16,128,512]{2,1,0:T(8,128)S(1)} %fusion.121, f32[16,512,128]{1,2,0:T(8,128)S(1)} %copy-done.17), kind=kOutput, calls=%fused_computation.410 | convolution fusion | flops 6449266688 | bytes 12582916 | tf_op jit(solution)/shard_map/kx,vzx...->vzk.../dot_general | solution.py:37
  539.0 9.5 pmax.14
  557.7 9.5 all-reduce.3
  570.5 19.2 %fusion.13 = (f32[64,128,128]{2,0,1:T(8,128)}, f32[64,128,128]{2,0,1:T(8,128)}) fusion(f32[128,128,64]{1,2,0:T(8,128)} %convolution_subtract_fusion, f32[128,128,64]{1,2,0:T(8,128)} %convolution_add_fusion, f32[128]{0:T(128)S(1)} %broadcast_multiply_fusion.3, f32[64,128]{0,1:T(8,128)S(1)} %add_multiply_fusion.1), kind=kLoop, calls=%fused_computation.17 | loop fusion | flops 7340032 | bytes 16810496 | tf_op jit(solution)/shard_map/reduce_sum | solution.py:87
  589.7 175.1 %all-reduce.7.cloned.1.call-done = (f32[64,128,128]{2,0,1:T(8,128)}, f32[64,128,128]{2,0,1:T(8,128)}) async-done(((f32[64,128,128]{2,0,1:T(8,128)}, f32[64,128,128]{2,0,1:T(8,128)}), (f32[64,128,128]{2,0,1:T(8,128)}, f32[64,128,128]{2,0,1:T(8,128)})) %all-reduce.7.cloned.1.call-update) | async-done | bytes 8388624 | tf_op jit(solution)/shard_map/psum | solution.py:87
  764.8 10.4 fusion.24
  775.2 8.4 fusion.18
  783.7 6.3 fusion.16
  796.2 6.4 add_bitcast_fusion.3
  802.7 7.1 fusion.60
  809.8 8.2 add_bitcast_fusion.2
  823.2 8.8 fusion.62
  832.0 8.2 subtract_bitcast_fusion.2
  840.2 30.2 %all-to-all-done.5 = f32[1,64,128,128]{3,2,0,1:T(8,128)} async-done(((f32[1,64,128,128]{3,2,0,1:T(8,128)}), f32[1,64,128,128]{3,2,0,1:T(8,128)}, u32[]{:S(2)}, u32[]{:S(2)}) %all-to-all-start.5) | async-done | bytes 4194336 | tf_op jit(solution)/shard_map/all_to_all | solution.py:69
  886.0 36.3 %all-to-all-done.4 = f32[1,64,128,128]{3,2,0,1:T(8,128)} async-done(((f32[1,64,128,128]{3,2,0,1:T(8,128)}), f32[1,64,128,128]{3,2,0,1:T(8,128)}, u32[]{:S(2)}, u32[]{:S(2)}) %all-to-all-start.4) | async-done | bytes 4194336 | tf_op jit(solution)/shard_map/all_to_all | solution.py:68
  933.2 12.9 %fusion.119 = f32[16,128,512]{2,1,0:T(8,128)S(1)} fusion(f32[16,512,128]{1,2,0:T(8,128)} %reshape.469), kind=kOutput, calls=%fused_computation.133 | convolution fusion | flops 6446120960 | bytes 8388608 | tf_op jit(solution)/shard_map/kx,vzx...->vzk.../dot_general | solution.py:37
  946.1 13.1 %fusion.408 = (f32[]{:T(128)}, f32[16,128,512]{2,1,0:T(8,128)}) fusion(f32[16,128,512]{2,1,0:T(8,128)S(1)} %fusion.119, f32[16,512,128]{1,2,0:T(8,128)S(1)} %copy-done.18), kind=kOutput, calls=%fused_computation.411 | convolution fusion | flops 6449266688 | bytes 12582916 | tf_op jit(solution)/shard_map/kx,vzx...->vzk.../dot_general | solution.py:37
  959.2 9.5 pmax.15
  977.9 9.5 all-reduce.2
  990.8 21.9 %fusion.141 = f32[128,128,64]{1,2,0:T(8,128)S(1)} fusion(f32[128,128,64]{1,2,0:T(8,128)} %convolution_subtract_fusion, f32[128,128,64]{1,2,0:T(8,128)} %convolution_add_fusion, f32[128]{0:T(128)S(1)} %broadcast_multiply_fusion, f32[64,128]{0,1:T(8,128)S(1)} %add_multiply_fusion), kind=kOutput, calls=%fused_computation.144 | convolution fusion | flops 809558016 | bytes 12616192 | tf_op jit(solution)/shard_map/kz,vz...->vk.../dot_general | solution.py:33
  1012.8 19.8 %fusion.139 = f32[128,128,64]{1,2,0:T(8,128)S(1)} fusion(f32[128,128,64]{1,2,0:T(8,128)S(1)} %copy-done.1, f32[128,128,64]{1,2,0:T(8,128)S(1)} %copy-done, f32[128]{0:T(128)S(1)} %broadcast_multiply_fusion, f32[64,128]{0,1:T(8,128)S(1)} %add_multiply_fusion), kind=kOutput, calls=%fused_computation.143 | convolution fusion | flops 809558016 | bytes 12616192 | tf_op jit(solution)/shard_map/kz,vz...->vk.../dot_general | solution.py:33
  1032.6 19.6 %subtract_bitcast_fusion.1 = f32[64,128,128]{2,0,1:T(8,128)S(1)} fusion(f32[128,128,64]{1,2,0:T(8,128)S(1)} %fusion.141, f32[128,128,64]{1,2,0:T(8,128)S(1)} %copy-done.1, f32[128,128,64]{1,2,0:T(8,128)S(1)} %copy-done, f32[128]{0:T(128)S(1)} %broadcast_multiply_fusion, f32[64,128]{0,1:T(8,128)S(1)} %add_multiply_fusion), kind=kOutput, calls=%fused_computation.64 | convolution fusion | flops 810606592 | bytes 16810496 | tf_op jit(solution)/shard_map/kz,vz...->vk.../dot_general | solution.py:33
  1052.2 20.1 %add_bitcast_fusion.1 = f32[64,128,128]{2,0,1:T(8,128)S(1)} fusion(f32[128,128,64]{1,2,0:T(8,128)S(1)} %fusion.139, f32[128,128,64]{1,2,0:T(8,128)S(1)} %copy-done.1, f32[128,128,64]{1,2,0:T(8,128)S(1)} %copy-done, f32[128]{0:T(128)S(1)} %broadcast_multiply_fusion, f32[64,128]{0,1:T(8,128)S(1)} %add_multiply_fusion), kind=kOutput, calls=%fused_computation.63 | convolution fusion | flops 810606592 | bytes 16810496 | tf_op jit(solution)/shard_map/kz,vz...->vk.../dot_general | solution.py:33
  1072.4 7.0 fusion.52
  1079.4 8.2 add_bitcast_fusion
  1092.7 8.8 fusion.54
  1101.5 8.2 subtract_bitcast_fusion
  1109.7 25.1 %all-to-all-done.7 = f32[1,64,128,128]{3,2,0,1:T(8,128)} async-done(((f32[1,64,128,128]{3,2,0,1:T(8,128)}), f32[1,64,128,128]{3,2,0,1:T(8,128)}, u32[]{:S(2)}, u32[]{:S(2)}) %all-to-all-start.7) | async-done | bytes 4194336 | tf_op jit(solution)/shard_map/all_to_all | solution.py:69
  1150.4 36.2 %all-to-all-done.6 = f32[1,64,128,128]{3,2,0,1:T(8,128)} async-done(((f32[1,64,128,128]{3,2,0,1:T(8,128)}), f32[1,64,128,128]{3,2,0,1:T(8,128)}, u32[]{:S(2)}, u32[]{:S(2)}) %all-to-all-start.6) | async-done | bytes 4194336 | tf_op jit(solution)/shard_map/all_to_all | solution.py:68
  1197.5 12.9 %fusion.117 = f32[16,128,512]{2,1,0:T(8,128)S(1)} fusion(f32[16,512,128]{1,2,0:T(8,128)} %reshape.475), kind=kOutput, calls=%fused_computation.131 | convolution fusion | flops 6446120960 | bytes 8388608 | tf_op jit(solution)/shard_map/kx,vzx...->vzk.../dot_general | solution.py:37
  1210.5 12.5 %multiply_bitcast_fusion = f32[1,16,512,128]{2,3,1,0:T(8,128)} fusion(f32[16,128,512]{2,1,0:T(8,128)S(1)} %fusion.117, f32[16,512,128]{1,2,0:T(8,128)S(1)} %copy-done.15), kind=kOutput, calls=%fused_computation.60 | convolution fusion | flops 6448218112 | bytes 12582912 | tf_op jit(solution)/shard_map/kx,vzx...->vzk.../dot_general | solution.py:37
  (108 shorter events, 193.5 us)
Async XLA Ops:
  7.2 13.2 %copy-start.5 = (f32[1,16,512,128]{3,2,1,0:T(8,128)S(1)}, f32[1,16,512,128]{3,2,1,0:T(8,128)}, u32[]{:S(2)}) copy-start(f32[1,16,512,128]{3,2,1,0:T(8,128)} %param.1) | copy-start | bytes 12582916
  20.4 11.1 copy-start.4
  31.5 4.2 copy-start.2
  44.0 54.0 %all-to-all-start = ((f32[1,16,512,128]{3,1,0,2:T(8,128)}), f32[1,16,512,128]{3,1,0,2:T(8,128)}, u32[]{:S(2)}, u32[]{:S(2)}) async-start(f32[1,16,512,128]{3,1,0,2:T(8,128)} %copy.24), calls=%async_computation | async-start | bytes 8388608 | tf_op jit(solution)/shard_map/all_to_all | solution.py:51
  49.4 6.0 copy-start.3
  98.0 52.0 %all-to-all-start.1 = ((f32[1,16,512,128]{3,1,0,2:T(8,128)}), f32[1,16,512,128]{3,1,0,2:T(8,128)}, u32[]{:S(2)}, u32[]{:S(2)}) async-start(f32[1,16,512,128]{3,1,0,2:T(8,128)} %copy.26), calls=%async_computation.1 | async-start | bytes 8388608 | tf_op jit(solution)/shard_map/all_to_all | solution.py:52
  103.0 241.4 %all-reduce.9.cloned.1.call-start = ((), (), s32[]{:S(2)}) async-start(), calls=%async_computation.9 | async-start | bytes 16777216 | tf_op jit(solution)/shard_map/psum | solution.py:87
  106.0 2.0 copy-start.8
  152.9 4.2 copy-start.16
  157.0 5.4 copy-start.9
  354.8 8.4 copy-start.21
  375.8 13.5 %copy-start.11 = (f32[64,128,128]{2,0,1:T(8,128)}, f32[64,128,128]{2,0,1:T(8,128)S(1)}, u32[]{:S(2)}) copy-start(f32[64,128,128]{2,0,1:T(8,128)S(1)} %subtract_bitcast_fusion.5) | copy-start | bytes 12582916
  382.2 7.1 copy-start.19
  397.5 52.6 %all-to-all-start.3 = ((f32[1,64,128,128]{3,2,0,1:T(8,128)}), f32[1,64,128,128]{3,2,0,1:T(8,128)}, u32[]{:S(2)}, u32[]{:S(2)}) async-start(f32[1,64,128,128]{3,2,0,1:T(8,128)} %add_bitcast_fusion.4), calls=%async_computation.3 | async-start | bytes 8388608 | tf_op jit(solution)/shard_map/all_to_all | solution.py:69
  402.8 8.8 copy-start.12
  450.1 51.9 %all-to-all-start.2 = ((f32[1,64,128,128]{3,2,0,1:T(8,128)}), f32[1,64,128,128]{3,2,0,1:T(8,128)}, u32[]{:S(2)}, u32[]{:S(2)}) async-start(f32[1,64,128,128]{3,2,0,1:T(8,128)} %subtract_bitcast_fusion.4), calls=%async_computation.2 | async-start | bytes 8388608 | tf_op jit(solution)/shard_map/all_to_all | solution.py:68
  455.1 309.8 %all-reduce.7.cloned.1.call-start = ((), (), s32[]{:S(2)}) async-start(), calls=%async_computation.8 | async-start | bytes 16777216 | tf_op jit(solution)/shard_map/psum | solution.py:87
  512.9 13.0 %copy-start.17 = (f32[16,512,128]{1,2,0:T(8,128)S(1)}, f32[16,512,128]{1,2,0:T(8,128)}, u32[]{:S(2)}) copy-start(f32[16,512,128]{1,2,0:T(8,128)} %reshape.464) | copy-start | bytes 12582916
  775.2 8.4 copy-start.22
  796.2 13.5 %copy-start.13 = (f32[64,128,128]{2,0,1:T(8,128)}, f32[64,128,128]{2,0,1:T(8,128)S(1)}, u32[]{:S(2)}) copy-start(f32[64,128,128]{2,0,1:T(8,128)S(1)} %subtract_bitcast_fusion.3) | copy-start | bytes 12582916
  802.7 7.1 copy-start.20
  818.0 52.4 %all-to-all-start.5 = ((f32[1,64,128,128]{3,2,0,1:T(8,128)}), f32[1,64,128,128]{3,2,0,1:T(8,128)}, u32[]{:S(2)}, u32[]{:S(2)}) async-start(f32[1,64,128,128]{3,2,0,1:T(8,128)} %add_bitcast_fusion.2), calls=%async_computation.5 | async-start | bytes 8388608 | tf_op jit(solution)/shard_map/all_to_all | solution.py:69
  823.2 8.8 copy-start.14
  870.4 51.9 %all-to-all-start.4 = ((f32[1,64,128,128]{3,2,0,1:T(8,128)}), f32[1,64,128,128]{3,2,0,1:T(8,128)}, u32[]{:S(2)}, u32[]{:S(2)}) async-start(f32[1,64,128,128]{3,2,0,1:T(8,128)} %subtract_bitcast_fusion.2), calls=%async_computation.4 | async-start | bytes 8388608 | tf_op jit(solution)/shard_map/all_to_all | solution.py:68
  933.2 13.0 %copy-start.18 = (f32[16,512,128]{1,2,0:T(8,128)S(1)}, f32[16,512,128]{1,2,0:T(8,128)}, u32[]{:S(2)}) copy-start(f32[16,512,128]{1,2,0:T(8,128)} %reshape.470) | copy-start | bytes 12582916
  988.1 24.6 %copy-start.23 = (f32[1,3]{1,0:T(1,128)}, f32[1,3]{1,0:T(1,128)S(1)}, u32[]{:S(2)}) copy-start(f32[1,3]{1,0:T(1,128)S(1)} %broadcast_divide_fusion) | copy-start | bytes 40
  990.8 21.9 %copy-start = (f32[128,128,64]{1,2,0:T(8,128)S(1)}, f32[128,128,64]{1,2,0:T(8,128)}, u32[]{:S(2)}) copy-start(f32[128,128,64]{1,2,0:T(8,128)} %convolution_add_fusion) | copy-start | bytes 12582916
  990.8 21.9 %copy-start.1 = (f32[128,128,64]{1,2,0:T(8,128)S(1)}, f32[128,128,64]{1,2,0:T(8,128)}, u32[]{:S(2)}) copy-start(f32[128,128,64]{1,2,0:T(8,128)} %convolution_subtract_fusion) | copy-start | bytes 12582916
  1052.2 27.2 %copy-start.6 = (f32[64,128,128]{2,0,1:T(8,128)}, f32[64,128,128]{2,0,1:T(8,128)S(1)}, u32[]{:S(2)}) copy-start(f32[64,128,128]{2,0,1:T(8,128)S(1)} %subtract_bitcast_fusion.1) | copy-start | bytes 12582916
  1072.3 7.1 copy-start.10
  1087.6 47.1 %all-to-all-start.7 = ((f32[1,64,128,128]{3,2,0,1:T(8,128)}), f32[1,64,128,128]{3,2,0,1:T(8,128)}, u32[]{:S(2)}, u32[]{:S(2)}) async-start(f32[1,64,128,128]{3,2,0,1:T(8,128)} %add_bitcast_fusion), calls=%async_computation.7 | async-start | bytes 8388608 | tf_op jit(solution)/shard_map/all_to_all | solution.py:69
  1092.7 8.8 copy-start.7
  1134.8 51.8 %all-to-all-start.6 = ((f32[1,64,128,128]{3,2,0,1:T(8,128)}), f32[1,64,128,128]{3,2,0,1:T(8,128)}, u32[]{:S(2)}, u32[]{:S(2)}) async-start(f32[1,64,128,128]{3,2,0,1:T(8,128)} %subtract_bitcast_fusion), calls=%async_computation.6 | async-start | bytes 8388608 | tf_op jit(solution)/shard_map/all_to_all | solution.py:68
  1197.5 13.0 %copy-start.15 = (f32[16,512,128]{1,2,0:T(8,128)S(1)}, f32[16,512,128]{1,2,0:T(8,128)}, u32[]{:S(2)}) copy-start(f32[16,512,128]{1,2,0:T(8,128)} %reshape.476) | copy-start | bytes 12582916
Sparse Core Ops, SparseCore 0:
  168.4 175.9 all-reduce.8
  589.8 174.9 all-reduce.6
where the time goes:
time: 1250 us; the launch traced here: 1240 us
  waiting for transfers between devices  617 us (49%)
  matrix products  373 us (30%)
  local copies, waits for them, and re-layouts  87.9 us (7%)
  other arithmetic  59.8 us (5%)
  starting transfers between devices  40.9 us (3%)
  blocking collectives  38 us (3%)
  between operations  19.1 us (2%)
    psum x2, waiting for transfers between devices, template_sum(): lax.psum((jnp.sum(spectrum[0], axis=0), jnp.sum(spectrum[1], axis=0)), 'tm')  351 us
    dot_general x16, matrix products, mix_z(): return jnp.einsum('kz,vz...->vk...', table, data, precision=precise)  157 us
    dot_general x16, matrix products, mix_y(): return jnp.dot(data, table, precision=precise)  115 us
    all_to_all x3, waiting for transfers between devices, inverse(): lax.all_to_all(real_y, 'space', split_axis=1, concat_axis=2, tiled=True)  109 us
    dot_general x8, matrix products, mix_x(): return jnp.einsum('kx,vzx...->vzk...', table, data, precision=precise)  102 us
    all_to_all x3, waiting for transfers between devices, inverse(): lax.all_to_all(imag_y, 'space', split_axis=1, concat_axis=2, tiled=True)  85.7 us
    all_to_all x1, waiting for transfers between devices, forward(): lax.all_to_all(imag_y, 'space', split_axis=2, concat_axis=1, tiled=True)  36.6 us
    all_to_all x1, waiting for transfers between devices, forward(): lax.all_to_all(real_y, 'space', split_axis=2, concat_axis=1, tiled=True)  34.3 us
  transfers between devices with their start and end apart: 10, of which 10 were waited for; matrix products, arithmetic and copies ran while one was open for 9% of the time, Pallas kernels for 0%

commit v1 on v0

--- a/solution.py
+++ b/solution.py
@@ -11,6 +11,18 @@
 precise = lax.Precision.HIGHEST
 sharpness = 256.0
 floor_share = 0.05
+
+
+def exchange_directly(x, axis, split, join):
+    ways, here = (lax.axis_size(axis), lax.axis_index(axis))
+    width = x.shape[split] // ways
+    turned = jnp.roll(x, -here * width, axis=split)
+    got = [lax.slice_in_dim(turned, 0, width, axis=split)]
+    for far in range(1, ways):
+        sent = lax.slice_in_dim(turned, far * width, (far + 1) * width, axis=split)
+        got.append(lax.ppermute(sent, axis, [(d, (d + far) % ways) for d in range(ways)]))
+    line = jnp.concatenate(got[::-1], axis=join)
+    return jnp.roll(line, (here + 1) * got[0].shape[join], axis=join)
 
 
 def dft_tables(length):
@@ -66,7 +78,7 @@
     imag_y = mix_y(real_z, sin_y) + mix_y(imag_z, cos_y)
     real_s, imag_s = (
         lax.all_to_all(real_y, "space", split_axis=1, concat_axis=2, tiled=True),
-        lax.all_to_all(imag_y, "space", split_axis=1, concat_axis=2, tiled=True),
+        exchange_directly(imag_y, "space", 1, 2),
     )
     return (mix_x(cos_x, real_s) - mix_x(sin_x, imag_s)) * norming
 

time: 1250 us -> 1190 us (0.952)
  waiting for transfers between devices: 617 us -> 554 us
  matrix products: 373 us -> 403 us
  local copies, waits for them, and re-layouts: 87.9 us -> 59.7 us
    all_to_all x3 -> x0, waiting for transfers between devices: 85.7 us -> none  [inverse(): lax.all_to_all(imag_y, 'space', split_axis=1, concat_axis=2, tiled=True)]
    ppermute x0 -> x9, waiting for transfers between devices: none -> 53.5 us  [exchange_directly(): lax.ppermute(sent, axis, [(d, (d + far) % ways) for d in range(ways)])]
    dot_general x8, matrix products: 102 us -> 135 us  [mix_x(): return jnp.einsum('kx,vzx...->vzk...', table, data, precision=precise)]
    all_to_all x3, waiting for transfers between devices: 109 us -> 77.7 us  [inverse(): lax.all_to_all(real_y, 'space', split_axis=1, concat_axis=2, tiled=True)]
    another operation x6 -> x3, local copies, waits for them, and re-layouts: 33.2 us -> 17.1 us
    all_to_all x3 -> x0, local copies, waits for them, and re-layouts: 15.8 us -> none  [inverse(): lax.all_to_all(imag_y, 'space', split_axis=1, concat_axis=2, tiled=True)]
    all_to_all x3 -> x0, starting transfers between devices: 15.5 us -> none  [inverse(): lax.all_to_all(imag_y, 'space', split_axis=1, concat_axis=2, tiled=True)]
  transfers between devices with their start and end apart: 10 -> 16, of which waited for: 10 -> 10; matrix products, arithmetic and copies ran while one was open for 9% -> 13% of each run, Pallas kernels for 0% -> 0%
where the time goes in v1:
time: 1190 us; the launch traced here: 1180 us
  waiting for transfers between devices  554 us (47%)
  matrix products  403 us (34%)
  other arithmetic  64.8 us (5%)
  local copies, waits for them, and re-layouts  59.7 us (5%)
  blocking collectives  40.2 us (3%)
  starting transfers between devices  37.9 us (3%)
  between operations  19 us (2%)
    psum x2, waiting for transfers between devices, template_sum(): lax.psum((jnp.sum(spectrum[0], axis=0), jnp.sum(spectrum[1], axis=0)), 'tm')  352 us
    dot_general x16, matrix products, mix_z(): return jnp.einsum('kz,vz...->vk...', table, data, precision=precise)  157 us
    dot_general x8, matrix products, mix_x(): return jnp.einsum('kx,vzx...->vzk...', table, data, precision=precise)  135 us
    dot_general x16, matrix products, mix_y(): return jnp.dot(data, table, precision=precise)  111 us
    all_to_all x3, waiting for transfers between devices, inverse(): lax.all_to_all(real_y, 'space', split_axis=1, concat_axis=2, tiled=True)  77.7 us
    ppermute x9, waiting for transfers between devices, exchange_directly(): lax.ppermute(sent, axis, [(d, (d + far) % ways) for d in range(ways)])  53.5 us
    all_to_all x1, waiting for transfers between devices, forward(): lax.all_to_all(imag_y, 'space', split_axis=2, concat_axis=1, tiled=True)  36.6 us
    all_to_all x1, waiting for transfers between devices, forward(): lax.all_to_all(real_y, 'space', split_axis=2, concat_axis=1, tiled=True)  34.3 us
  transfers between devices with their start and end apart: 16, of which 10 were waited for; matrix products, arithmetic and copies ran while one was open for 13% of the time, Pallas kernels for 0%

profile of v1, /device:TPU:0, one launch (start us, length us, event | category | flops | bytes accessed | tf_op | source)
XLA Modules:
  0.0 1179.5 jit_solution(2725954101040737801)
XLA Ops:
  7.2 13.2 %fusion.82 = f32[512,16,128]{2,0,1:T(8,128)S(1)} fusion(f32[1,16,512,128]{3,2,1,0:T(8,128)} %param.5), kind=kOutput, calls=%fused_computation.118 | convolution fusion | flops 6446120960 | bytes 8388608 | tf_op jit(solution)/shard_map/kx,vzx...->vzk.../dot_general | solution.py:49
  20.4 11.1 fusion.80
  63.7 34.3 %all-to-all-done = f32[1,16,512,128]{3,1,0,2:T(8,128)} async-done(((f32[1,16,512,128]{3,1,0,2:T(8,128)}), f32[1,16,512,128]{3,1,0,2:T(8,128)}, u32[]{:S(2)}, u32[]{:S(2)}) %all-to-all-start) | async-done | bytes 4194336 | tf_op jit(solution)/shard_map/all_to_all | solution.py:63
  113.4 36.6 %all-to-all-done.1 = f32[1,16,512,128]{3,1,0,2:T(8,128)} async-done(((f32[1,16,512,128]{3,1,0,2:T(8,128)}), f32[1,16,512,128]{3,1,0,2:T(8,128)}, u32[]{:S(2)}, u32[]{:S(2)}) %all-to-all-start.1) | async-done | bytes 4194336 | tf_op jit(solution)/shard_map/all_to_all | solution.py:64
  168.3 176.1 %all-reduce.9.cloned.1.call-done = (f32[64,128,128]{2,0,1:T(8,128)}, f32[64,128,128]{2,0,1:T(8,128)}) async-done(((f32[64,128,128]{2,0,1:T(8,128)}, f32[64,128,128]{2,0,1:T(8,128)}), (f32[64,128,128]{2,0,1:T(8,128)}, f32[64,128,128]{2,0,1:T(8,128)})) %all-reduce.9.cloned.1.call-update) | async-done | bytes 8388624 | tf_op jit(solution)/shard_map/psum | solution.py:99
  344.4 10.4 fusion.70
  354.8 8.4 fusion.64
  363.2 6.3 fusion.62
  369.6 6.2 subtract_bitcast_fusion.5
  375.8 6.6 add_bitcast_fusion.5
  382.4 7.1 fusion.106
  389.5 8.2 subtract_bitcast_fusion.4
  402.9 8.7 fusion.104
  411.6 7.1 add_bitcast_fusion.4
  425.7 25.9 %all-to-all-done.2 = f32[1,64,128,128]{3,2,0,1:T(8,128)} async-done(((f32[1,64,128,128]{3,2,0,1:T(8,128)}), f32[1,64,128,128]{3,2,0,1:T(8,128)}, u32[]{:S(2)}, u32[]{:S(2)}) %all-to-all-start.2) | async-done | bytes 4194336 | tf_op jit(solution)/shard_map/all_to_all | solution.py:80
  462.6 13.4 %fusion.163 = f32[16,128,512]{2,1,0:T(8,128)S(1)} fusion(f32[16,512,128]{1,2,0:T(8,128)} %reshape.460), kind=kOutput, calls=%fused_computation.195 | convolution fusion | flops 6446120960 | bytes 8388608 | tf_op jit(solution)/shard_map/kx,vzx...->vzk.../dot_general | solution.py:49
  476.1 19.9 %collective-permute-done.2 = f32[1,16,128,128]{3,2,1,0:T(8,128)} collective-permute-done((f32[1,16,128,128]{3,2,1,0:T(8,128)S(1)}, f32[1,16,128,128]{3,2,1,0:T(8,128)}, u32[]{:S(2)}, u32[]{:S(2)}) %collective-permute-start.2) | collective-permute-done | bytes 1048608 | tf_op jit(solution)/shard_map/ppermute | solution.py:23
  496.0 23.5 %fusion.455 = (f32[]{:T(128)}, f32[16,128,512]{2,1,0:T(8,128)}) fusion(f32[16,128,512]{2,1,0:T(8,128)S(1)} %fusion.163, s32[]{:T(128)S(6)} %select_n.238, f32[1,16,128,128]{3,2,1,0:T(8,128)} %collective-permute-done, f32[1,16,128,128]{3,2,1,0:T(8,128)} %collective-permute-done.1, f32[1,16,128,128]{3,2,1,0:T(8,128)} %collective-permute-done.2, ...), kind=kOutput, calls=%fused_computation.476 | convolution fusion | flops 6456606720 | bytes 12582920 | tf_op jit(solution)/shard_map/kx,vzx...->vzk.../dot_general | solution.py:49
  519.5 12.1 %pmax.14 = f32[]{:T(128)} all-reduce(f32[]{:T(128)} %get-tuple-element.50), channel_id=1, replica_groups=mesh['tm'=8,'space'=4] {'space'}, use_global_device_ids=true, to_apply=%region_3.6 | all-reduce | flops 1 | bytes 8 | tf_op jit(solution)/shard_map/pmax | solution.py:113
  540.8 8.1 all-reduce.3
  552.2 19.2 %fusion.13 = (f32[64,128,128]{2,0,1:T(8,128)}, f32[64,128,128]{2,0,1:T(8,128)}) fusion(f32[128,128,64]{1,2,0:T(8,128)} %convolution_subtract_fusion, f32[128,128,64]{1,2,0:T(8,128)} %convolution_add_fusion, f32[128]{0:T(128)S(1)} %broadcast_multiply_fusion.3, f32[64,128]{0,1:T(8,128)S(1)} %add_multiply_fusion.1), kind=kLoop, calls=%fused_computation.47 | loop fusion | flops 7340032 | bytes 16810496 | tf_op jit(solution)/shard_map/reduce_sum | solution.py:99
  571.4 176.3 %all-reduce.7.cloned.1.call-done = (f32[64,128,128]{2,0,1:T(8,128)}, f32[64,128,128]{2,0,1:T(8,128)}) async-done(((f32[64,128,128]{2,0,1:T(8,128)}, f32[64,128,128]{2,0,1:T(8,128)}), (f32[64,128,128]{2,0,1:T(8,128)}, f32[64,128,128]{2,0,1:T(8,128)})) %all-reduce.7.cloned.1.call-update) | async-done | bytes 8388624 | tf_op jit(solution)/shard_map/psum | solution.py:99
  747.7 10.4 fusion.60
  758.1 8.4 fusion.54
  766.5 6.3 fusion.52
  779.1 6.6 add_bitcast_fusion.3
  785.7 7.1 fusion.98
  792.8 8.2 subtract_bitcast_fusion.2
  805.9 8.9 fusion.96
  814.8 7.1 add_bitcast_fusion.2
  828.9 25.8 %all-to-all-done.3 = f32[1,64,128,128]{3,2,0,1:T(8,128)} async-done(((f32[1,64,128,128]{3,2,0,1:T(8,128)}), f32[1,64,128,128]{3,2,0,1:T(8,128)}, u32[]{:S(2)}, u32[]{:S(2)}) %all-to-all-start.3) | async-done | bytes 4194336 | tf_op jit(solution)/shard_map/all_to_all | solution.py:80
  865.6 13.4 %fusion.161 = f32[16,128,512]{2,1,0:T(8,128)S(1)} fusion(f32[16,512,128]{1,2,0:T(8,128)} %reshape.466), kind=kOutput, calls=%fused_computation.193 | convolution fusion | flops 6446120960 | bytes 8388608 | tf_op jit(solution)/shard_map/kx,vzx...->vzk.../dot_general | solution.py:49
  879.0 20.1 %collective-permute-done.5 = f32[1,16,128,128]{3,2,1,0:T(8,128)} collective-permute-done((f32[1,16,128,128]{3,2,1,0:T(8,128)S(1)}, f32[1,16,128,128]{3,2,1,0:T(8,128)}, u32[]{:S(2)}, u32[]{:S(2)}) %collective-permute-start.5) | collective-permute-done | bytes 1048608 | tf_op jit(solution)/shard_map/ppermute | solution.py:23
  899.1 23.8 %fusion.456 = (f32[]{:T(128)}, f32[16,128,512]{2,1,0:T(8,128)}) fusion(f32[16,128,512]{2,1,0:T(8,128)S(1)} %fusion.161, s32[]{:T(128)S(6)} %select_n.238, f32[1,16,128,128]{3,2,1,0:T(8,128)} %collective-permute-done.3, f32[1,16,128,128]{3,2,1,0:T(8,128)} %collective-permute-done.4, f32[1,16,128,128]{3,2,1,0:T(8,128)} %collective-permute-done.5, ...), kind=kOutput, calls=%fused_computation.477 | convolution fusion | flops 6456606720 | bytes 12582920 | tf_op jit(solution)/shard_map/kx,vzx...->vzk.../dot_general | solution.py:49
  922.9 11.9 %pmax.15 = f32[]{:T(128)} all-reduce(f32[]{:T(128)} %get-tuple-element.52), channel_id=1, replica_groups=mesh['tm'=8,'space'=4] {'space'}, use_global_device_ids=true, to_apply=%region_16.19 | all-reduce | flops 1 | bytes 8 | tf_op jit(solution)/shard_map/pmax | solution.py:113
  944.0 8.1 all-reduce.2
  955.4 21.9 %fusion.183 = f32[128,128,64]{1,2,0:T(8,128)S(1)} fusion(f32[128,128,64]{1,2,0:T(8,128)} %convolution_subtract_fusion, f32[128,128,64]{1,2,0:T(8,128)} %convolution_add_fusion, f32[128]{0:T(128)S(1)} %get-tuple-element.54, f32[64,128]{0,1:T(8,128)S(1)} %add_multiply_fusion), kind=kOutput, calls=%fused_computation.204 | convolution fusion | flops 809558016 | bytes 12616192 | tf_op jit(solution)/shard_map/kz,vz...->vk.../dot_general | solution.py:45
  977.4 19.6 %fusion.181 = f32[128,128,64]{1,2,0:T(8,128)S(1)} fusion(f32[128,128,64]{1,2,0:T(8,128)S(1)} %copy-done.1, f32[128,128,64]{1,2,0:T(8,128)S(1)} %copy-done, f32[128]{0:T(128)S(1)} %get-tuple-element.54, f32[64,128]{0,1:T(8,128)S(1)} %add_multiply_fusion), kind=kOutput, calls=%fused_computation.203 | convolution fusion | flops 809558016 | bytes 12616192 | tf_op jit(solution)/shard_map/kz,vz...->vk.../dot_general | solution.py:45
  997.0 19.9 %subtract_bitcast_fusion.1 = f32[64,128,128]{2,0,1:T(8,128)S(1)} fusion(f32[128,128,64]{1,2,0:T(8,128)S(1)} %fusion.183, f32[128,128,64]{1,2,0:T(8,128)S(1)} %copy-done.1, f32[128,128,64]{1,2,0:T(8,128)S(1)} %copy-done, f32[128]{0:T(128)S(1)} %get-tuple-element.54, f32[64,128]{0,1:T(8,128)S(1)} %add_multiply_fusion), kind=kOutput, calls=%fused_computation.124 | convolution fusion | flops 810606592 | bytes 16810496 | tf_op jit(solution)/shard_map/kz,vz...->vk.../dot_general | solution.py:45
  1016.9 19.9 %add_bitcast_fusion.1 = f32[64,128,128]{2,0,1:T(8,128)S(1)} fusion(f32[128,128,64]{1,2,0:T(8,128)S(1)} %fusion.181, f32[128,128,64]{1,2,0:T(8,128)S(1)} %copy-done.1, f32[128,128,64]{1,2,0:T(8,128)S(1)} %copy-done, f32[128]{0:T(128)S(1)} %get-tuple-element.54, f32[64,128]{0,1:T(8,128)S(1)} %add_multiply_fusion), kind=kOutput, calls=%fused_computation.123 | convolution fusion | flops 810606592 | bytes 16810496 | tf_op jit(solution)/shard_map/kz,vz...->vk.../dot_general | solution.py:45
  1036.8 7.1 fusion.90
  1043.9 8.2 subtract_bitcast_fusion
  1057.4 8.7 fusion.88
  1066.1 7.1 add_bitcast_fusion
  1080.2 26.0 %all-to-all-done.4 = f32[1,64,128,128]{3,2,0,1:T(8,128)} async-done(((f32[1,64,128,128]{3,2,0,1:T(8,128)}), f32[1,64,128,128]{3,2,0,1:T(8,128)}, u32[]{:S(2)}, u32[]{:S(2)}) %all-to-all-start.4) | async-done | bytes 4194336 | tf_op jit(solution)/shard_map/all_to_all | solution.py:80
  1117.0 13.4 %fusion.159 = f32[16,128,512]{2,1,0:T(8,128)S(1)} fusion(f32[16,512,128]{1,2,0:T(8,128)} %reshape.472), kind=kOutput, calls=%fused_computation.191 | convolution fusion | flops 6446120960 | bytes 8388608 | tf_op jit(solution)/shard_map/kx,vzx...->vzk.../dot_general | solution.py:49
  1130.5 13.5 %collective-permute-done.8 = f32[1,16,128,128]{3,2,1,0:T(8,128)} collective-permute-done((f32[1,16,128,128]{3,2,1,0:T(8,128)S(1)}, f32[1,16,128,128]{3,2,1,0:T(8,128)}, u32[]{:S(2)}, u32[]{:S(2)}) %collective-permute-start.8) | collective-permute-done | bytes 1048608 | tf_op jit(solution)/shard_map/ppermute | solution.py:23
  1143.9 23.0 %multiply_bitcast_fusion = f32[1,16,512,128]{2,3,1,0:T(8,128)} fusion(f32[16,128,512]{2,1,0:T(8,128)S(1)} %fusion.159, s32[]{:T(128)S(6)} %select_n.238, f32[1,16,128,128]{3,2,1,0:T(8,128)} %collective-permute-done.6, f32[1,16,128,128]{3,2,1,0:T(8,128)} %collective-permute-done.7, f32[1,16,128,128]{3,2,1,0:T(8,128)} %collective-permute-done.8, ...), kind=kOutput, calls=%fused_computation.120 | convolution fusion | flops 6455558144 | bytes 12582916 | tf_op jit(solution)/shard_map/kx,vzx...->vzk.../dot_general | solution.py:49
  (113 shorter events, 167.4 us)
Async XLA Ops:
  7.2 13.2 %copy-start.5 = (f32[1,16,512,128]{3,2,1,0:T(8,128)S(1)}, f32[1,16,512,128]{3,2,1,0:T(8,128)}, u32[]{:S(2)}) copy-start(f32[1,16,512,128]{3,2,1,0:T(8,128)} %param.5) | copy-start | bytes 12582916
  20.4 11.1 copy-start.4
  31.5 4.2 copy-start.2
  44.0 54.0 %all-to-all-start = ((f32[1,16,512,128]{3,1,0,2:T(8,128)}), f32[1,16,512,128]{3,1,0,2:T(8,128)}, u32[]{:S(2)}, u32[]{:S(2)}) async-start(f32[1,16,512,128]{3,1,0,2:T(8,128)} %copy.42), calls=%async_computation | async-start | bytes 8388608 | tf_op jit(solution)/shard_map/all_to_all | solution.py:63
  49.4 6.0 copy-start.3
  98.0 52.0 %all-to-all-start.1 = ((f32[1,16,512,128]{3,1,0,2:T(8,128)}), f32[1,16,512,128]{3,1,0,2:T(8,128)}, u32[]{:S(2)}, u32[]{:S(2)}) async-start(f32[1,16,512,128]{3,1,0,2:T(8,128)} %copy.44), calls=%async_computation.1 | async-start | bytes 8388608 | tf_op jit(solution)/shard_map/all_to_all | solution.py:64
  103.0 241.4 %all-reduce.9.cloned.1.call-start = ((), (), s32[]{:S(2)}) async-start(), calls=%async_computation.6 | async-start | bytes 16777216 | tf_op jit(solution)/shard_map/psum | solution.py:99
  106.0 2.0 copy-start.8
  152.9 4.2 copy-start.15
  157.0 5.4 copy-start.9
  354.8 8.4 copy-start.18
  375.8 13.7 %copy-start.11 = (f32[64,128,128]{2,0,1:T(8,128)}, f32[64,128,128]{2,0,1:T(8,128)S(1)}, u32[]{:S(2)}) copy-start(f32[64,128,128]{2,0,1:T(8,128)S(1)} %subtract_bitcast_fusion.5) | copy-start | bytes 12582916
  382.4 7.1 copy-start.16
  397.8 53.8 %all-to-all-start.2 = ((f32[1,64,128,128]{3,2,0,1:T(8,128)}), f32[1,64,128,128]{3,2,0,1:T(8,128)}, u32[]{:S(2)}, u32[]{:S(2)}) async-start(f32[1,64,128,128]{3,2,0,1:T(8,128)} %subtract_bitcast_fusion.4), calls=%async_computation.2 | async-start | bytes 8388608 | tf_op jit(solution)/shard_map/all_to_all | solution.py:80
  402.8 344.9 %all-reduce.7.cloned.1.call-start = ((), (), s32[]{:S(2)}) async-start(), calls=%async_computation.5 | async-start | bytes 16777216 | tf_op jit(solution)/shard_map/psum | solution.py:99
  402.9 8.7 copy-start.12
  421.6 54.4 %collective-permute-start = (f32[1,16,128,128]{3,2,1,0:T(8,128)}, f32[1,16,128,128]{3,2,1,0:T(8,128)}, u32[]{:S(2)}, u32[]{:S(2)}) collective-permute-start(f32[1,16,128,128]{3,2,1,0:T(8,128)} %get-tuple-element.43), channel_id=1, source_target_pairs={{0,3},{1,0},{2,1},{3,2},{4,7},{5,4},{6,5},{7,6},{8,11},{9,8},{10,9... | collective-permute-start | bytes 3145736 | tf_op jit(solution)/shard_map/ppermute | solution.py:23
  424.5 51.5 %collective-permute-start.1 = (f32[1,16,128,128]{3,2,1,0:T(8,128)S(1)}, f32[1,16,128,128]{3,2,1,0:T(8,128)}, u32[]{:S(2)}, u32[]{:S(2)}) collective-permute-start(f32[1,16,128,128]{3,2,1,0:T(8,128)S(1)} %get-tuple-element.42), channel_id=1, source_target_pairs={{0,2},{1,3},{2,0},{3,1},{4,6},{5,7},{6,4},{7,5},{8,10},{9,11},{10,... | collective-permute-start | bytes 3145736 | tf_op jit(solution)/shard_map/ppermute | solution.py:23
  425.1 70.9 %collective-permute-start.2 = (f32[1,16,128,128]{3,2,1,0:T(8,128)S(1)}, f32[1,16,128,128]{3,2,1,0:T(8,128)}, u32[]{:S(2)}, u32[]{:S(2)}) collective-permute-start(f32[1,16,128,128]{3,2,1,0:T(8,128)S(1)} %get-tuple-element.41), channel_id=1, source_target_pairs={{0,1},{1,2},{2,3},{3,0},{4,5},{5,6},{6,7},{7,4},{8,9},{9,10},{10,1... | collective-permute-start | bytes 3145736 | tf_op jit(solution)/shard_map/ppermute | solution.py:23
  758.1 8.4 copy-start.19
  779.1 13.7 %copy-start.13 = (f32[64,128,128]{2,0,1:T(8,128)}, f32[64,128,128]{2,0,1:T(8,128)S(1)}, u32[]{:S(2)}) copy-start(f32[64,128,128]{2,0,1:T(8,128)S(1)} %subtract_bitcast_fusion.3) | copy-start | bytes 12582916
  785.7 7.1 copy-start.17
  801.1 53.6 %all-to-all-start.3 = ((f32[1,64,128,128]{3,2,0,1:T(8,128)}), f32[1,64,128,128]{3,2,0,1:T(8,128)}, u32[]{:S(2)}, u32[]{:S(2)}) async-start(f32[1,64,128,128]{3,2,0,1:T(8,128)} %subtract_bitcast_fusion.2), calls=%async_computation.3 | async-start | bytes 8388608 | tf_op jit(solution)/shard_map/all_to_all | solution.py:80
  805.9 8.9 copy-start.14
  824.9 54.1 %collective-permute-start.3 = (f32[1,16,128,128]{3,2,1,0:T(8,128)}, f32[1,16,128,128]{3,2,1,0:T(8,128)}, u32[]{:S(2)}, u32[]{:S(2)}) collective-permute-start(f32[1,16,128,128]{3,2,1,0:T(8,128)} %get-tuple-element.39), channel_id=1, source_target_pairs={{0,3},{1,0},{2,1},{3,2},{4,7},{5,4},{6,5},{7,6},{8,11},{9,8},{10,9... | collective-permute-start | bytes 3145736 | tf_op jit(solution)/shard_map/ppermute | solution.py:23
  827.7 51.3 %collective-permute-start.4 = (f32[1,16,128,128]{3,2,1,0:T(8,128)S(1)}, f32[1,16,128,128]{3,2,1,0:T(8,128)}, u32[]{:S(2)}, u32[]{:S(2)}) collective-permute-start(f32[1,16,128,128]{3,2,1,0:T(8,128)S(1)} %get-tuple-element.38), channel_id=1, source_target_pairs={{0,2},{1,3},{2,0},{3,1},{4,6},{5,7},{6,4},{7,5},{8,10},{9,11},{10,... | collective-permute-start | bytes 3145736 | tf_op jit(solution)/shard_map/ppermute | solution.py:23
  828.3 70.8 %collective-permute-start.5 = (f32[1,16,128,128]{3,2,1,0:T(8,128)S(1)}, f32[1,16,128,128]{3,2,1,0:T(8,128)}, u32[]{:S(2)}, u32[]{:S(2)}) collective-permute-start(f32[1,16,128,128]{3,2,1,0:T(8,128)S(1)} %get-tuple-element.37), channel_id=1, source_target_pairs={{0,1},{1,2},{2,3},{3,0},{4,5},{5,6},{6,7},{7,4},{8,9},{9,10},{10,1... | collective-permute-start | bytes 3145736 | tf_op jit(solution)/shard_map/ppermute | solution.py:23
  952.7 24.6 %copy-start.20 = (f32[1,3]{1,0:T(1,128)}, f32[1,3]{1,0:T(1,128)S(1)}, u32[]{:S(2)}) copy-start(f32[1,3]{1,0:T(1,128)S(1)} %broadcast_divide_fusion) | copy-start | bytes 40
  955.4 22.0 %copy-start = (f32[128,128,64]{1,2,0:T(8,128)S(1)}, f32[128,128,64]{1,2,0:T(8,128)}, u32[]{:S(2)}) copy-start(f32[128,128,64]{1,2,0:T(8,128)} %convolution_add_fusion) | copy-start | bytes 12582916
  955.4 22.0 %copy-start.1 = (f32[128,128,64]{1,2,0:T(8,128)S(1)}, f32[128,128,64]{1,2,0:T(8,128)}, u32[]{:S(2)}) copy-start(f32[128,128,64]{1,2,0:T(8,128)} %convolution_subtract_fusion) | copy-start | bytes 12582916
  1016.9 27.0 %copy-start.6 = (f32[64,128,128]{2,0,1:T(8,128)}, f32[64,128,128]{2,0,1:T(8,128)S(1)}, u32[]{:S(2)}) copy-start(f32[64,128,128]{2,0,1:T(8,128)S(1)} %subtract_bitcast_fusion.1) | copy-start | bytes 12582916
  1036.8 7.1 copy-start.10
  1052.1 54.1 %all-to-all-start.4 = ((f32[1,64,128,128]{3,2,0,1:T(8,128)}), f32[1,64,128,128]{3,2,0,1:T(8,128)}, u32[]{:S(2)}, u32[]{:S(2)}) async-start(f32[1,64,128,128]{3,2,0,1:T(8,128)} %subtract_bitcast_fusion), calls=%async_computation.4 | async-start | bytes 8388608 | tf_op jit(solution)/shard_map/all_to_all | solution.py:80
  1057.4 8.7 copy-start.7
  1076.2 54.3 %collective-permute-start.6 = (f32[1,16,128,128]{3,2,1,0:T(8,128)}, f32[1,16,128,128]{3,2,1,0:T(8,128)}, u32[]{:S(2)}, u32[]{:S(2)}) collective-permute-start(f32[1,16,128,128]{3,2,1,0:T(8,128)} %get-tuple-element.35), channel_id=1, source_target_pairs={{0,3},{1,0},{2,1},{3,2},{4,7},{5,4},{6,5},{7,6},{8,11},{9,8},{10,9... | collective-permute-start | bytes 3145736 | tf_op jit(solution)/shard_map/ppermute | solution.py:23
  1079.1 51.4 %collective-permute-start.7 = (f32[1,16,128,128]{3,2,1,0:T(8,128)S(1)}, f32[1,16,128,128]{3,2,1,0:T(8,128)}, u32[]{:S(2)}, u32[]{:S(2)}) collective-permute-start(f32[1,16,128,128]{3,2,1,0:T(8,128)S(1)} %get-tuple-element.34), channel_id=1, source_target_pairs={{0,2},{1,3},{2,0},{3,1},{4,6},{5,7},{6,4},{7,5},{8,10},{9,11},{10,... | collective-permute-start | bytes 3145736 | tf_op jit(solution)/shard_map/ppermute | solution.py:23
  1079.7 64.3 %collective-permute-start.8 = (f32[1,16,128,128]{3,2,1,0:T(8,128)S(1)}, f32[1,16,128,128]{3,2,1,0:T(8,128)}, u32[]{:S(2)}, u32[]{:S(2)}) collective-permute-start(f32[1,16,128,128]{3,2,1,0:T(8,128)S(1)} %get-tuple-element.33), channel_id=1, source_target_pairs={{0,1},{1,2},{2,3},{3,0},{4,5},{5,6},{6,7},{7,4},{8,9},{9,10},{10,1... | collective-permute-start | bytes 3145736 | tf_op jit(solution)/shard_map/ppermute | solution.py:23
Sparse Core Ops, SparseCore 0:
  168.4 175.9 all-reduce.8
  571.5 176.1 all-reduce.6
